TPU v7x, 512 devices: a whole 4x4x16 slice. The times are simulated.
512 devices in a mesh: mpo: 16 (over z), sec: 32 (over x, y, core).
Axes of the slice: x: 4, y: 4, z: 16, core: 2. Of those that a mesh axis runs over, the one named last changes fastest.
Arguments:
- environment: bfloat16 [48, 64, 128, 128], P('mpo', 'sec'), may hold values from -6 to 6
- site_tensor: bfloat16 [64, 4, 128, 128], P('sec'), may hold values from -0.25 to 0.25
- mpo_tensor: bfloat16 [48, 48, 4, 4], P('mpo'), may hold values from -0.75 to 0.75
- mpo_pattern: int32 [48, 48], P('mpo'), may hold values 0 or 1
- sector_rows: int32 [64], replicated, may hold values from 64 to 128
- sector_map: int32 [64], replicated, may hold values from 0 to 63, as said below
Outputs:
- new_environment: bfloat16 [48, 64, 128, 128], P('mpo', 'sec')
Inputs may be any that keep to these rules, and one draw needn't show every extreme that they name: A permutation of the 64 sector labels: sector g takes the new label sector_map[g].
All inputs are finite; a program needn't handle non-finite values. No bound on the sum of `mpo_pattern` on one device may be relied on, other than what follows from the above.
Results may differ from a plain program's by a relative error of at most 0.02.
Values may be sent and summed in bfloat16 or wider, within the bound.
No kernel may reach another device: no remote copies, remote signals or barrier semaphores. Data moves between devices by JAX's collectives and lax.ppermute only.
A program may use at most 64 MiB of HBM per device.

v0:
```python
import jax
import jax.numpy as jnp
from jax import lax
from jax.sharding import PartitionSpec as P


def per_device(environment, site_tensor, mpo_tensor, mpo_pattern, sector_rows, sector_map):
    per_dev = environment.shape[1]
    block = environment.shape[2]
    masked = jnp.where(mpo_pattern[:, :, None, None] != 0, mpo_tensor, jnp.zeros_like(mpo_tensor))
    left = jnp.einsum(
        "gsxa,bgxc->gbsac", site_tensor, environment, preferred_element_type=jnp.float32
    ).astype(jnp.bfloat16)
    sandwich = jnp.einsum(
        "gbsac,gtcz->bstgaz", left, site_tensor, preferred_element_type=jnp.float32
    ).astype(jnp.bfloat16)
    parts = jnp.einsum(
        "bpst,bstgaz->pgaz", masked, sandwich, preferred_element_type=jnp.float32
    ).astype(jnp.bfloat16)
    summed = lax.psum_scatter(parts, "mpo", scatter_dimension=0, tiled=True)
    device = lax.axis_index("sec")
    local = jnp.arange(per_dev, dtype=jnp.int32)
    own_labels = device * per_dev + local
    sizes = jnp.take(sector_rows, own_labels, axis=0)
    places = jnp.arange(block, dtype=jnp.int32)
    keep = (places[None, :, None] < sizes[:, None, None]) & (
        places[None, None, :] < sizes[:, None, None]
    )
    result = jnp.where(keep[None, :, :, :], summed, jnp.zeros_like(summed))
    gathered = lax.all_gather(result, "sec", axis=1, tiled=True)
    nsec = sector_map.shape[0]
    inverse = jnp.zeros((nsec,), jnp.int32).at[sector_map].set(jnp.arange(nsec, dtype=jnp.int32))
    source = jnp.take(inverse, own_labels, axis=0)
    return jnp.take(gathered, source, axis=1)


def solution(mesh):
    return jax.shard_map(
        per_device,
        mesh=mesh,
        in_specs=(
            P("mpo", "sec", None, None),
            P("sec", None, None, None),
            P("mpo", None, None, None),
            P("mpo", None),
            P(),
            P(),
        ),
        out_specs=P("mpo", "sec", None, None),
        check_vma=False,
    )
```

profile of v0, /device:TPU:1, one launch (start us, length us, event | category | flops | bytes accessed | tf_op | source)
XLA Modules:
  0.0 175.2 jit_solution(12927616610973831131)
XLA Ops:
  6.5 0.0 copy-start
  6.5 0.0 copy-start.2
  6.5 0.0 reduce-scatter.2.cloned.1.call-start
  6.5 0.7 broadcast_compare_fusion
  7.3 0.2 copy-done
  7.5 2.1 %convert_bitcast_fusion = bf16[3,4,4,2,128,128]{5,4,2,1,0,3:T(8,128)(2,1)S(1)} fusion(bf16[2,4,128,128]{3,2,1,0:T(8,128)(2,1)S(1)} %copy-done, bf16[3,2,128,128]{3,2,1,0:T(8,128)(2,1)} %param.8), kind=kOutput, calls=%fused_computation.7 | convolution fusion | flops 505282560 | bytes 3604480 | tf_op jit(solution)/shard_map/gbsac,gtcz->bstgaz/dot_general | solution.py:14
  9.7 0.0 copy-done.2
  9.7 4.0 %bitcast_convert_fusion = bf16[48,2,128,128]{3,0,2,1:T(8,128)(2,1)S(1)} fusion(bf16[3,4,4,2,128,128]{5,4,2,1,0,3:T(8,128)(2,1)S(1)} %convert_bitcast_fusion, bf16[3,48,4,4]{1,3,2,0:T(4,128)(2,1)S(1)} %copy-done.2, pred[3,48]{1,0:T(4,128)(4,1)S(1)} %broadcast_compare_fusion), kind=kOutput, calls=%fused_computation.4 | convolution fusion | flops 152570112 | bytes 6296208 | tf_op jit(solution)/shard_map/bpst,bstgaz->pgaz/dot_general | solution.py:17
  13.7 2.5 %copy.12 = bf16[48,2,128,128]{3,2,1,0:T(8,128)(2,1)} copy(bf16[48,2,128,128]{3,0,2,1:T(8,128)(2,1)S(1)} %bitcast_convert_fusion) | data formatting | bytes 6291456 | tf_op jit(solution)/shard_map/convert_element_type | solution.py:19
  16.2 0.0 copy-start.1
  16.2 0.0 copy-start.3
  16.2 0.0 reduce-scatter.2.cloned.1.call-update
  16.2 0.0 all-gather.2.cloned.1.call-start
  16.3 0.5 copy-done.1
  16.8 0.6 gather_fusion.2
  17.5 0.1 iota_compare_fusion
  17.6 0.1 broadcast_and_fusion
  17.7 71.9 %reduce-scatter.2.cloned.1.call-done = bf16[3,2,128,128]{3,2,1,0:T(8,128)(2,1)} async-done(((bf16[48,2,128,128]{3,2,1,0:T(8,128)(2,1)}), bf16[3,2,128,128]{3,2,1,0:T(8,128)(2,1)}) %reduce-scatter.2.cloned.1.call-update) | async-done | bytes 196624 | tf_op jit(solution)/shard_map/reduce_scatter | solution.py:20
  89.6 0.9 broadcast_select_fusion
  90.5 0.7 copy.13
  91.2 0.0 all-gather.2.cloned.1.call-update
  91.3 0.0 copy-done.3
  91.3 0.8 scatter_custom_fusion
  92.1 0.6 gather_fusion.1
  92.7 71.5 %all-gather.2.cloned.1.call-done = bf16[3,64,128,128]{3,2,0,1:T(8,128)(2,1)} async-done(((bf16[3,2,128,128]{3,2,0,1:T(8,128)(2,1)}), bf16[3,64,128,128]{3,2,0,1:T(8,128)(2,1)}) %all-gather.2.cloned.1.call-update) | async-done | bytes 6291472 | tf_op jit(solution)/shard_map/all_gather | solution.py:30
  164.2 3.4 %gather_fusion = bf16[2,3,128,128]{3,2,1,0:T(8,128)(2,1)S(1)} fusion(bf16[3,64,128,128]{3,2,0,1:T(8,128)(2,1)} %all-gather.2.cloned.1.call-done, s32[1024]{0:T(1024)S(1)} %pad_clamp_fusion), kind=kCustom, calls=%fused_computation.2 | custom fusion | bytes 393224 | tf_op jit(solution)/shard_map/jit(_take)/gather | solution.py:34
  167.6 0.1 select_bitcast_fusion
  167.7 0.7 copy.14
  (7 shorter events, 0.0 us)
Async XLA Ops:
  6.5 1.0 copy-start
  6.5 3.1 %copy-start.2 = (bf16[3,48,4,4]{1,3,2,0:T(4,128)(2,1)S(1)}, bf16[3,48,4,4]{1,3,2,0:T(4,128)(2,1)}, u32[]{:S(2)}) copy-start(bf16[3,48,4,4]{1,3,2,0:T(4,128)(2,1)} %param.10) | copy-start | bytes 13828
  6.5 83.1 %reduce-scatter.2.cloned.1.call-start = ((), (), s32[]{:S(2)}) async-start(), calls=%async_computation.1 | async-start | bytes 3342336 | tf_op jit(solution)/shard_map/reduce_scatter | solution.py:20
  16.2 0.7 copy-start.1
  16.2 75.1 %copy-start.3 = (s32[64]{0:T(128)S(1)}, s32[64]{0:T(128)}, u32[]{:S(2)}) copy-start(s32[64]{0:T(128)} %param.13) | copy-start | bytes 772
  16.2 148.0 %all-gather.2.cloned.1.call-start = ((), (), s32[]{:S(2)}) async-start(), calls=%async_computation.2 | async-start | bytes 6488064 | tf_op jit(solution)/shard_map/all_gather | solution.py:30
Sparse Core Ops, SparseCore 0:
  16.3 73.2 reduce-scatter.1
  92.7 71.4 all-gather.1
where the time goes:
time: 175 us
  waiting for transfers between devices  143 us (82%)
  between operations  13.5 us (8%)
  local copies, waits for them, and re-layouts  10.1 us (6%)
  matrix products  6.18 us (4%)
  other arithmetic  1.98 us (1%)
    reduce_scatter x1, waiting for transfers between devices, per_device(): summed = lax.psum_scatter(parts, 'mpo', scatter_dimension=0, tiled=True)  71.9 us
    all_gather x1, waiting for transfers between devices, per_device(): gathered = lax.all_gather(result, 'sec', axis=1, tiled=True)  71.5 us
    dot_general x1, matrix products, per_device(): jnp.einsum('bpst,bstgaz->pgaz', masked, sandwich, preferred_element_type=...  4.03 us
  transfers between devices with their start and end apart: 2, of which 2 were waited for; matrix products, arithmetic and copies ran while one was open for 1% of the time, Pallas kernels for 0%

commit v1 on v0

--- a/solution.py
+++ b/solution.py
@@ -27,7 +27,9 @@
         places[None, None, :] < sizes[:, None, None]
     )
     result = jnp.where(keep[None, :, :, :], summed, jnp.zeros_like(summed))
-    gathered = lax.all_gather(result, "sec", axis=1, tiled=True)
+    gathered = jnp.concatenate(
+        lax.all_to_all(jnp.stack([result] * lax.axis_size("sec")), "sec", 0, 0), axis=1
+    )
     nsec = sector_map.shape[0]
     inverse = jnp.zeros((nsec,), jnp.int32).at[sector_map].set(jnp.arange(nsec, dtype=jnp.int32))
     source = jnp.take(inverse, own_labels, axis=0)

time: 175 us -> 218 us (1.25)
  the two profiles are of different devices: /device:TPU:1 before, /device:TPU:8 now
where the time goes in v1:
time: 218 us
  waiting for transfers between devices  167 us (77%)
  local copies, waits for them, and re-layouts  21.7 us (10%)
  between operations  13.5 us (6%)
  starting transfers between devices  7.74 us (4%)
  matrix products  6.18 us (3%)
    all_to_all x1, waiting for transfers between devices, per_device(): lax.all_to_all(jnp.stack([result] * lax.axis_size('sec')), 'sec', 0, 0)  87 us
    reduce_scatter x1, waiting for transfers between devices, per_device(): summed = lax.psum_scatter(parts, 'mpo', scatter_dimension=0, tiled=True)  79.9 us
    all_to_all x1, local copies, waits for them, and re-layouts, per_device(): lax.all_to_all(jnp.stack([result] * lax.axis_size('sec')), 'sec', 0, 0)  8.07 us
    all_to_all x1, starting transfers between devices, per_device(): lax.all_to_all(jnp.stack([result] * lax.axis_size('sec')), 'sec', 0, 0)  7.74 us
  transfers between devices with their start and end apart: 2, of which 2 were waited for; matrix products, arithmetic and copies ran while one was open for 1% of the time, Pallas kernels for 0%

profile of v1, /device:TPU:8, one launch (start us, length us, event | category | flops | bytes accessed | tf_op | source)
XLA Modules:
  0.0 218.0 jit_solution(9052111344644544600)
XLA Ops:
  6.5 0.0 copy-start
  6.5 0.0 copy-start.2
  6.5 0.0 reduce-scatter.2.cloned.1.call-start
  6.5 0.7 broadcast_compare_fusion
  7.3 0.2 copy-done
  7.5 2.1 convert_bitcast_fusion
  9.7 0.0 copy-done.2
  9.7 4.0 %bitcast_convert_fusion = bf16[48,2,128,128]{3,0,2,1:T(8,128)(2,1)S(1)} fusion(bf16[3,4,4,2,128,128]{5,4,2,1,0,3:T(8,128)(2,1)S(1)} %convert_bitcast_fusion, bf16[3,48,4,4]{1,3,2,0:T(4,128)(2,1)S(1)} %copy-done.2, pred[3,48]{1,0:T(4,128)(4,1)S(1)} %broadcast_compare_fusion), kind=kOutput, calls=%fused_computation.4 | convolution fusion | flops 152570112 | bytes 6296208 | tf_op jit(solution)/shard_map/bpst,bstgaz->pgaz/dot_general | solution.py:17
  13.7 2.5 %copy.13 = bf16[48,2,128,128]{3,2,1,0:T(8,128)(2,1)} copy(bf16[48,2,128,128]{3,0,2,1:T(8,128)(2,1)S(1)} %bitcast_convert_fusion) | data formatting | bytes 6291456 | tf_op jit(solution)/shard_map/convert_element_type | solution.py:19
  16.2 0.0 copy-start.1
  16.2 0.0 reduce-scatter.2.cloned.1.call-update
  16.2 0.6 copy-done.1
  16.8 0.6 gather_fusion.2
  17.5 0.1 iota_compare_fusion
  17.6 0.1 broadcast_and_fusion
  17.7 79.9 %reduce-scatter.2.cloned.1.call-done = bf16[3,2,128,128]{3,2,1,0:T(8,128)(2,1)} async-done(((bf16[48,2,128,128]{3,2,1,0:T(8,128)(2,1)}), bf16[3,2,128,128]{3,2,1,0:T(8,128)(2,1)}) %reduce-scatter.2.cloned.1.call-update) | async-done | bytes 196624 | tf_op jit(solution)/shard_map/reduce_scatter | solution.py:20
  97.5 0.9 broadcast_select_fusion
  98.5 4.2 %stack.2 = bf16[32,3,2,128,128]{4,3,2,1,0:T(8,128)(2,1)} broadcast(bf16[3,2,128,128]{3,2,1,0:T(8,128)(2,1)S(1)} %broadcast_select_fusion), dimensions={1,2,3,4} | broadcast | bytes 6488064 | tf_op jit(solution)/shard_map/stack | solution.py:31
  102.7 0.0 copy-start.3
  102.7 7.7 %all-to-all-start = ((bf16[32,3,2,128,128]{4,3,2,1,0:T(8,128)(2,1)}), bf16[32,3,2,128,128]{4,3,2,1,0:T(8,128)(2,1)}, u32[]{:S(2)}, u32[]{:S(2)}) async-start(bf16[32,3,2,128,128]{4,3,2,1,0:T(8,128)(2,1)} %stack.2), calls=%async_computation.1 | async-start | bytes 12582912 | tf_op jit(solution)/shard_map/all_to_all | solution.py:31
  110.5 0.0 copy-done.3
  110.5 0.8 scatter_custom_fusion
  111.3 0.6 gather_fusion.1
  112.0 87.0 %all-to-all-done = bf16[32,3,2,128,128]{4,3,2,1,0:T(8,128)(2,1)} async-done(((bf16[32,3,2,128,128]{4,3,2,1,0:T(8,128)(2,1)}), bf16[32,3,2,128,128]{4,3,2,1,0:T(8,128)(2,1)}, u32[]{:S(2)}, u32[]{:S(2)}) %all-to-all-start) | async-done | bytes 6291488 | tf_op jit(solution)/shard_map/all_to_all | solution.py:31
  199.0 8.1 %copy.14 = bf16[32,3,2,128,128]{4,3,2,0,1:T(8,128)(2,1)} copy(bf16[32,3,2,128,128]{4,3,2,1,0:T(8,128)(2,1)} %all-to-all-done) | data formatting | bytes 12582912 | tf_op jit(solution)/shard_map/all_to_all | solution.py:31
  207.0 3.4 %gather_fusion = bf16[2,3,128,128]{3,2,1,0:T(8,128)(2,1)S(1)} fusion(bf16[3,64,128,128]{3,2,1,0:T(8,128)(2,1)} %bitcast.41, s32[1024]{0:T(1024)S(1)} %pad_clamp_fusion), kind=kCustom, calls=%fused_computation.2 | custom fusion | bytes 393224 | tf_op jit(solution)/shard_map/jit(_take)/gather | solution.py:36
  210.4 0.1 select_bitcast_fusion
  210.5 0.7 copy.15
  (7 shorter events, 0.0 us)
Async XLA Ops:
  6.5 1.0 copy-start
  6.5 3.1 %copy-start.2 = (bf16[3,48,4,4]{1,3,2,0:T(4,128)(2,1)S(1)}, bf16[3,48,4,4]{1,3,2,0:T(4,128)(2,1)}, u32[]{:S(2)}) copy-start(bf16[3,48,4,4]{1,3,2,0:T(4,128)(2,1)} %param.10) | copy-start | bytes 13828
  6.5 91.0 %reduce-scatter.2.cloned.1.call-start = ((), (), s32[]{:S(2)}) async-start(), calls=%async_computation.2 | async-start | bytes 3342336 | tf_op jit(solution)/shard_map/reduce_scatter | solution.py:20
  16.2 0.7 copy-start.1
  102.7 7.8 %copy-start.3 = (s32[64]{0:T(128)S(1)}, s32[64]{0:T(128)}, u32[]{:S(2)}) copy-start(s32[64]{0:T(128)} %param.13) | copy-start | bytes 772
  102.7 96.2 %all-to-all-start = ((bf16[32,3,2,128,128]{4,3,2,1,0:T(8,128)(2,1)}), bf16[32,3,2,128,128]{4,3,2,1,0:T(8,128)(2,1)}, u32[]{:S(2)}, u32[]{:S(2)}) async-start(bf16[32,3,2,128,128]{4,3,2,1,0:T(8,128)(2,1)} %stack.2), calls=%async_computation.1 | async-start | bytes 12582912 | tf_op jit(solution)/shard_map/all_to_all | solution.py:31
Sparse Core Ops, SparseCore 0:
  16.3 81.1 reduce-scatter.1
